TPU v7x, 256 devices: a whole 4x4x8 slice. The times are simulated.
256 devices in a mesh: gx: 16 (over x, y), gy: 16 (over z, core).
Axes of the slice: x: 4, y: 4, z: 8, core: 2. Of those that a mesh axis runs over, the one named last changes fastest.
Arguments:
- inv_factors: float32 [64, 64, 4096], P('gx', 'gy'), as said below
- couplings: float32 [64, 64, 2, 4096], P('gx', 'gy'), may hold values from -1.5 to 1.5
- stencil: int32 [64, 64, 2], P('gx', 'gy'), may hold values from 0 to 1
- coarse: int32 [64, 64], P('gx', 'gy'), may hold values from 0 to 1, as said below
Outputs:
- strength: float32 [64, 64, 2], P('gx', 'gy')
- restriction: bfloat16 [3072, 14, 4096], P(('gx', 'gy'))
Inputs may be any that keep to these rules, and one draw needn't show every extreme that they name: Each block of inv_factors is lower triangular with diagonal entries between 0.5 and 1. Each tile of 4 x 4 elements has at most 12 coarse elements, and some tile has exactly 12.
All inputs are finite; a program needn't handle non-finite values.
Results may differ from a plain program's by a relative error of at most 0.001.
Values sent between devices are 32-bit elements; how exact they have to be, the bound alone decides.
No kernel may reach another device: no remote copies, remote signals or barrier semaphores. Data moves between devices by JAX's collectives and lax.ppermute only.
A program may use at most 64 MiB of HBM per device.

v0:
```python
import math

import jax
import jax.numpy as jnp
from jax import lax
from jax.sharding import PartitionSpec as P

CAP = 12


def extended(cells, sides, width):
    for axis, dim in sides:
        count = lax.axis_size(axis)
        ends = count - 1
        head = lax.slice_in_dim(cells, 0, width, axis=dim)
        tail = lax.slice_in_dim(cells, cells.shape[dim] - width, cells.shape[dim], axis=dim)
        cells = jnp.concatenate(
            [
                lax.ppermute(tail, axis, [(i, (i + 1) % count) for i in range(ends)]),
                cells,
                lax.ppermute(head, axis, [((i + 1) % count, i) for i in range(ends)]),
            ],
            axis=dim,
        )
    return cells


def matmul(left_block, right_block):
    return jnp.einsum(
        "...ij,...jk->...ik", left_block, right_block, precision=lax.Precision.HIGHEST
    )


def left_gram(left_block, right_block):
    return jnp.einsum(
        "...ji,...jk->...ik", left_block, right_block, precision=lax.Precision.HIGHEST
    )


def right_gram(left_block, right_block):
    return jnp.einsum(
        "...ij,...kj->...ik", left_block, right_block, precision=lax.Precision.HIGHEST
    )


def crop_cycle(values, margin):
    return values[margin : values.shape[0] - margin, margin : values.shape[1] - margin]


def upwind_pick(values, upwind_side):
    trailing = (1,) * (values.ndim - 2)
    sign_x = upwind_side[:, :, 0].reshape(upwind_side.shape[:2] + trailing)
    sign_y = upwind_side[:, :, 1].reshape(upwind_side.shape[:2] + trailing)
    upwind_x = jnp.where(sign_x == 1, values[2:, 1:-1], values[:-2, 1:-1])
    upwind_y = jnp.where(sign_y == 1, values[1:-1, 2:], values[1:-1, :-2])
    return (upwind_x, upwind_y)


def near_paths(fine_inverse, minus_coupling, upwind_side):
    upwind_x, upwind_y = upwind_pick(fine_inverse, crop_cycle(upwind_side, 1))
    middle = crop_cycle(fine_inverse, 1)
    local_coupling = crop_cycle(minus_coupling, 1)
    step_x = matmul(local_coupling[:, :, 0], upwind_x)
    step_y = matmul(local_coupling[:, :, 1], upwind_y)
    return jnp.stack([middle, matmul(middle, step_x), matmul(middle, step_y)], axis=2)


def far_paths(fine_inverse, minus_coupling, upwind_side, near):
    upwind_x, upwind_y = upwind_pick(near, crop_cycle(upwind_side, 2))
    middle = crop_cycle(fine_inverse, 2)
    local_coupling = crop_cycle(minus_coupling, 2)
    lead_x = matmul(middle, local_coupling[:, :, 0])[:, :, None]
    lead_y = matmul(middle, local_coupling[:, :, 1])[:, :, None]
    return jnp.concatenate(
        [middle[:, :, None], matmul(lead_x, upwind_x), matmul(lead_y, upwind_y)], axis=2
    )


def strength_of(factor_cycle, minus_coupling, upwind_side):
    upwind_x, upwind_y = upwind_pick(factor_cycle, upwind_side)
    own_block = crop_cycle(factor_cycle, 1)
    result = []
    for direction, upwind_factor in ((0, upwind_x), (1, upwind_y)):
        scaled = right_gram(matmul(own_block, minus_coupling[:, :, direction]), upwind_factor)
        result.append(jnp.mean(scaled * scaled, axis=(-2, -1)))
    return jnp.stack(result, axis=-1)


def restriction_rows(paths_cycle, minus_coupling, upwind_side, coarse, capacity):
    upwind_x, upwind_y = upwind_pick(paths_cycle, upwind_side)
    cell_count = coarse.shape[0] * coarse.shape[1]
    flat_coarse = coarse.reshape(cell_count)
    slot_rank = jnp.cumsum(flat_coarse, dtype=jnp.int32) - flat_coarse
    chosen = (
        (slot_rank[None, :] == jnp.arange(capacity, dtype=jnp.int32)[:, None])
        & (flat_coarse[None, :] == 1)
    ).astype(jnp.int32)
    source = jnp.sum(
        chosen * jnp.arange(cell_count, dtype=jnp.int32)[None, :], axis=1, dtype=jnp.int32
    )
    filled = jnp.sum(chosen, axis=1, dtype=jnp.int32)
    rows_x = jnp.take(upwind_x.reshape((cell_count,) + upwind_x.shape[2:]), source, axis=0)
    rows_y = jnp.take(upwind_y.reshape((cell_count,) + upwind_y.shape[2:]), source, axis=0)
    coupling_rows = jnp.take(
        minus_coupling.reshape((cell_count,) + minus_coupling.shape[2:]), source, axis=0
    )
    restrict = jnp.concatenate(
        [matmul(coupling_rows[:, 0:1], rows_x), matmul(coupling_rows[:, 1:2], rows_y)], axis=1
    )
    restrict = (restrict * filled[:, None, None, None].astype(restrict.dtype)).astype(jnp.bfloat16)
    return restrict.reshape(restrict.shape[:2] + (restrict.shape[2] * restrict.shape[3],))


def on_device(inv_factors, couplings, stencil, coarse):
    rows_x, rows_y, flat_size = inv_factors.shape
    order = math.isqrt(flat_size)
    total_x = rows_x * lax.axis_size("gx")
    total_y = rows_y * lax.axis_size("gy")
    coord_x = lax.axis_index("gx") * rows_x + jnp.arange(rows_x, dtype=jnp.int32)
    coord_y = lax.axis_index("gy") * rows_y + jnp.arange(rows_y, dtype=jnp.int32)
    target_x = coord_x[:, None] + 2 * stencil[:, :, 0] - 1
    target_y = coord_y[None, :] + 2 * stencil[:, :, 1] - 1
    reach = jnp.stack(
        [(target_x >= 0) & (target_x < total_x), (target_y >= 0) & (target_y < total_y)], axis=-1
    )
    signed_mask = -reach.astype(jnp.float32)
    minus_own = (couplings * signed_mask[:, :, :, None]).reshape(rows_x, rows_y, 2, order, order)
    factor_own = inv_factors.reshape(rows_x, rows_y, order, order)
    stencil_codes = stencil[:, :, 0] + 2 * stencil[:, :, 1] + 4 * coarse
    cycle_depth = 2
    fine_own = (1 - coarse).astype(jnp.float32)[:, :, None, None] * left_gram(
        factor_own, factor_own
    )
    packed = jnp.concatenate([factor_own[:, :, None], fine_own[:, :, None], minus_own], axis=2)
    cycle_blocks = extended(packed, (("gx", 0), ("gy", 1)), cycle_depth)
    code_cycle = extended(stencil_codes, (("gx", 0), ("gy", 1)), cycle_depth)
    upwind_side = jnp.stack([code_cycle % 2, code_cycle // 2 % 2], axis=-1)
    factor_cycle = cycle_blocks[:, :, 0]
    fine_inverse = cycle_blocks[:, :, 1]
    coupling_cycle = cycle_blocks[:, :, 2:4]
    near = near_paths(fine_inverse, coupling_cycle, upwind_side)
    far = far_paths(fine_inverse, coupling_cycle, upwind_side, near)
    paths_cycle = extended(far, (("gx", 0), ("gy", 1)), 1)
    strong = strength_of(crop_cycle(factor_cycle, cycle_depth - 1), minus_own, stencil)
    restrict = restriction_rows(paths_cycle, minus_own, stencil, coarse, CAP)
    return (strong, restrict)


def solution(mesh):
    placed = (P("gx", "gy", None), P("gx", "gy", None, None), P("gx", "gy", None), P("gx", "gy"))
    return jax.shard_map(
        on_device,
        mesh=mesh,
        in_specs=placed,
        out_specs=(P("gx", "gy", None), P(("gx", "gy"), None, None)),
        check_vma=False,
    )
```

profile of v0, /device:TPU:103, one launch (start us, length us, event | category | flops | bytes accessed | tf_op | source)
XLA Modules:
  0.0 184.4 jit_solution(10979747378759755457)
XLA Ops:
  0.6 1.2 reshape.516
  1.9 1.3 broadcast_in_dim_reshape.4
  3.1 0.8 fusion.77
  4.3 1.3 broadcast_multiply_fusion
  5.6 0.8 copy-done.4
  6.8 0.5 reshape.517
  7.4 1.0 fusion.27
  8.6 1.5 fusion.75
  10.0 4.9 %collective-permute-start.1 = (f32[2,4,4,64,64]{4,3,1,0,2:T(8,128)}, f32[2,4,4,64,64]{4,3,1,0,2:T(8,128)S(1)}, u32[]{:S(2)}, u32[]{:S(2)}) collective-permute-start(f32[2,4,4,64,64]{4,3,1,0,2:T(8,128)} %get-tuple-element.22), channel_id=1, source_target_pairs={{16,0},{32,16},{48,32},{64,48},{80,64},{96,80},{112,96},{128,112},... | collective-permute-start | bytes 1572872 | tf_op jit(solution)/shard_map/ppermute | solution.py:21
  15.0 1.9 %collective-permute-start = (f32[2,4,4,64,64]{4,3,1,0,2:T(8,128)}, f32[2,4,4,64,64]{4,3,1,0,2:T(8,128)}, u32[]{:S(2)}, u32[]{:S(2)}) collective-permute-start(f32[2,4,4,64,64]{4,3,1,0,2:T(8,128)} %get-tuple-element.21), channel_id=1, source_target_pairs={{0,16},{16,32},{32,48},{48,64},{64,80},{80,96},{96,112},{112,128},... | collective-permute-start | bytes 1572872 | tf_op jit(solution)/shard_map/ppermute | solution.py:19
  16.9 5.5 %collective-permute-start.5 = (s32[2,4]{1,0:T(2,128)S(1)}, s32[2,4]{1,0:T(2,128)S(1)}, u32[]{:S(2)}, u32[]{:S(2)}) collective-permute-start(s32[2,4]{1,0:T(2,128)S(1)} %get-tuple-element.30), channel_id=1, source_target_pairs={{16,0},{32,16},{48,32},{64,48},{80,64},{96,80},{112,96},{128,112},... | collective-permute-start | bytes 104 | tf_op jit(solution)/shard_map/ppermute | solution.py:21
  22.4 1.9 %collective-permute-start.4 = (s32[2,4]{1,0:T(2,128)S(1)}, s32[2,4]{1,0:T(2,128)S(1)}, u32[]{:S(2)}, u32[]{:S(2)}) collective-permute-start(s32[2,4]{1,0:T(2,128)S(1)} %get-tuple-element.29), channel_id=1, source_target_pairs={{0,16},{16,32},{32,48},{48,64},{64,80},{80,96},{96,112},{112,128},... | collective-permute-start | bytes 104 | tf_op jit(solution)/shard_map/ppermute | solution.py:19
  24.8 2.6 %reshape_reshape.3 = f32[16,2,64,64]{3,2,1,0:T(8,128)} reshape(f32[4,4,2,4096]{3,2,1,0:T(2,128)} %copy-done.4) | data formatting | bytes 1048576 | tf_op jit(solution)/shard_map/reshape;reshape | solution.py:105
  27.4 2.7 %gather_fusion = f32[12,2,64,64]{3,2,1,0:T(8,128)} fusion(f32[16,2,64,64]{3,2,1,0:T(8,128)} %reshape_reshape.3, s32[1024]{0:T(1024)S(1)} %pad_clamp_fusion), kind=kCustom, calls=%fused_computation.2 | custom fusion | bytes 786480 | tf_op jit(solution)/shard_map/jit(_take)/gather | solution.py:104
  30.1 2.1 %copy_select_fusion = f32[12,2,64,64]{3,2,0,1:T(8,128)} fusion(f32[12,2,64,64]{3,2,1,0:T(8,128)} %gather_fusion, pred[12]{0:T(512)(128)(4,1)S(1)} %compare_and_fusion), kind=kLoop, calls=%fused_computation.98 | loop fusion | flops 98304 | bytes 786444 | tf_op jit(solution)/shard_map/jit(_take)/select_n | solution.py:104
  32.3 4.8 %collective-permute-done.1 = f32[2,4,4,64,64]{4,3,1,0,2:T(8,128)S(1)} collective-permute-done((f32[2,4,4,64,64]{4,3,1,0,2:T(8,128)}, f32[2,4,4,64,64]{4,3,1,0,2:T(8,128)S(1)}, u32[]{:S(2)}, u32[]{:S(2)}) %collective-permute-start.1) | collective-permute-done | bytes 524320 | tf_op jit(solution)/shard_map/ppermute | solution.py:21
  37.1 5.9 %collective-permute-done = f32[2,4,4,64,64]{4,3,1,0,2:T(8,128)} collective-permute-done((f32[2,4,4,64,64]{4,3,1,0,2:T(8,128)}, f32[2,4,4,64,64]{4,3,1,0,2:T(8,128)}, u32[]{:S(2)}, u32[]{:S(2)}) %collective-permute-start) | collective-permute-done | bytes 524320 | tf_op jit(solution)/shard_map/ppermute | solution.py:19
  43.0 1.7 pad_maximum_fusion.1
  44.7 2.3 %fusion.74 = (f32[8,2,4,64,64]{4,3,1,0,2:T(8,128)}, f32[8,2,4,64,64]{4,3,1,0,2:T(8,128)}) fusion(f32[8,4,4,64,64]{4,3,1,0,2:T(8,128)S(1)} %pad_maximum_fusion.1), kind=kLoop, calls=%fused_computation.163 | loop fusion | bytes 4194304 | tf_op jit(solution)/shard_map/slice | solution.py:16
  47.0 3.7 %collective-permute-start.3 = (f32[8,2,4,64,64]{4,3,1,0,2:T(8,128)}, f32[8,2,4,64,64]{4,3,1,0,2:T(8,128)}, u32[]{:S(2)}, u32[]{:S(2)}) collective-permute-start(f32[8,2,4,64,64]{4,3,1,0,2:T(8,128)} %get-tuple-element.16), channel_id=1, source_target_pairs={{1,0},{2,1},{3,2},{4,3},{5,4},{6,5},{7,6},{8,7},{9,8},{10,9},{11,1... | collective-permute-start | bytes 3145736 | tf_op jit(solution)/shard_map/ppermute | solution.py:21
  50.7 4.7 %collective-permute-start.2 = (f32[8,2,4,64,64]{4,3,1,0,2:T(8,128)}, f32[8,2,4,64,64]{4,3,1,0,2:T(8,128)}, u32[]{:S(2)}, u32[]{:S(2)}) collective-permute-start(f32[8,2,4,64,64]{4,3,1,0,2:T(8,128)} %get-tuple-element.15), channel_id=1, source_target_pairs={{0,1},{1,2},{2,3},{3,4},{4,5},{5,6},{6,7},{7,8},{8,9},{9,10},{10,1... | collective-permute-start | bytes 3145736 | tf_op jit(solution)/shard_map/ppermute | solution.py:19
  55.8 1.9 %collective-permute-start.7 = (s32[8,2]{1,0:T(8,128)S(1)}, s32[8,2]{1,0:T(8,128)S(1)}, u32[]{:S(2)}, u32[]{:S(2)}) collective-permute-start(s32[8,2]{1,0:T(8,128)S(1)} %get-tuple-element.26), channel_id=1, source_target_pairs={{1,0},{2,1},{3,2},{4,3},{5,4},{6,5},{7,6},{8,7},{9,8},{10,9},{11,1... | collective-permute-start | bytes 200 | tf_op jit(solution)/shard_map/ppermute | solution.py:21
  57.7 4.9 %collective-permute-start.6 = (s32[8,2]{1,0:T(8,128)S(1)}, s32[8,2]{1,0:T(8,128)S(1)}, u32[]{:S(2)}, u32[]{:S(2)}) collective-permute-start(s32[8,2]{1,0:T(8,128)S(1)} %get-tuple-element.25), channel_id=1, source_target_pairs={{0,1},{1,2},{2,3},{3,4},{4,5},{5,6},{6,7},{7,8},{8,9},{9,10},{10,1... | collective-permute-start | bytes 200 | tf_op jit(solution)/shard_map/ppermute | solution.py:19
  62.6 14.9 %collective-permute-done.7 = s32[8,2]{1,0:T(8,128)S(1)} collective-permute-done((s32[8,2]{1,0:T(8,128)S(1)}, s32[8,2]{1,0:T(8,128)S(1)}, u32[]{:S(2)}, u32[]{:S(2)}) %collective-permute-start.7) | collective-permute-done | bytes 96 | tf_op jit(solution)/shard_map/ppermute | solution.py:21
  77.6 1.1 collective-permute-done.6
  79.4 3.2 %pad_maximum_fusion = f32[8,8,4,64,64]{4,3,1,0,2:T(8,128)S(1)} fusion(f32[8,2,4,64,64]{4,3,1,0,2:T(8,128)} %collective-permute-done.3, f32[2,4,4,64,64]{4,3,1,0,2:T(8,128)S(1)} %collective-permute-done.1, f32[4,4,2,64,64]{4,3,1,0,2:T(8,128)S(1)} %reshape.517, f32[4,4,1,64,64]{4,3,1,0,2:T(8,128)S(1)} %fusion.27, ...), kind=kLoop, calls=%fused_computation.3 | loop fusion | flops 6291456 | bytes 8388608 | tf_op jit(solution)/shard_map/concatenate | solution.py:17
  82.6 0.7 fusion.63
  83.3 0.5 slice_bitcast_fusion
  83.8 1.5 fusion.62
  85.4 1.4 convolution_bitcast_fusion.2
  86.8 1.5 convolution_bitcast_fusion.3
  88.3 1.1 slice_bitcast_fusion.2
  89.4 0.8 slice_bitcast_fusion.3
  90.2 1.1 fusion.57
  91.3 2.5 %fusion.28 = f32[6,6,64,64]{3,2,1,0:T(8,128)S(1)} fusion(f32[8,8,64,64]{3,2,1,0:T(8,128)S(1)} %get-tuple-element.11, f32[8,2,4,64,64]{4,3,1,0,2:T(8,128)} %collective-permute-done.3, f32[8,2,4,64,64]{4,3,1,0,2:T(8,128)} %collective-permute-done.2, f32[2,4,4,64,64]{4,3,1,0,2:T(8,128)S(1)} %collective-permute-done.1, ...), kind=kOutput, calls=%fused_computation.61 | convolution fusion | flops 114278400 | bytes 8717312 | tf_op jit(solution)/shard_map/...ij,...jk->...ik/dot_general | solution.py:29
  93.8 2.3 %convolution_bitcast_fusion = f32[6,6,1,64,64]{4,3,1,0,2:T(8,128)} fusion(f32[6,6,64,64]{3,2,1,0:T(8,128)S(1)} %fusion.28, f32[8,8,4,64,64]{4,3,1,0,2:T(8,128)S(1)} %pad_maximum_fusion), kind=kOutput, calls=%fused_computation.43 | convolution fusion | flops 113246208 | bytes 3866624 | tf_op jit(solution)/shard_map/...ij,...jk->...ik/dot_general | solution.py:29
  96.2 2.5 %fusion.42 = f32[6,6,64,64]{3,2,1,0:T(8,128)S(1)} fusion(f32[8,8,64,64]{3,2,1,0:T(8,128)S(1)} %get-tuple-element.11, f32[8,2,4,64,64]{4,3,1,0,2:T(8,128)} %collective-permute-done.3, f32[8,2,4,64,64]{4,3,1,0,2:T(8,128)} %collective-permute-done.2, f32[2,4,4,64,64]{4,3,1,0,2:T(8,128)S(1)} %collective-permute-done.1, ...), kind=kOutput, calls=%fused_computation.77 | convolution fusion | flops 114278400 | bytes 8717312 | tf_op jit(solution)/shard_map/...ij,...jk->...ik/dot_general | solution.py:29
  98.7 2.4 %convolution_bitcast_fusion.1 = f32[6,6,1,64,64]{4,3,1,0,2:T(8,128)} fusion(f32[6,6,64,64]{3,2,1,0:T(8,128)S(1)} %fusion.42, f32[8,8,4,64,64]{4,3,1,0,2:T(8,128)S(1)} %pad_maximum_fusion), kind=kOutput, calls=%fused_computation.44 | convolution fusion | flops 113246208 | bytes 3866624 | tf_op jit(solution)/shard_map/...ij,...jk->...ik/dot_general | solution.py:29
  101.1 1.0 copy.67
  102.1 1.9 %pad_maximum_fusion.18 = f32[6,6,3,64,64]{4,3,1,0,2:T(8,128)S(1)} fusion(f32[6,6,1,64,64]{4,3,1,0,2:T(8,128)S(1)} %copy-done.10, f32[6,6,1,64,64]{4,3,1,0,2:T(8,128)} %convolution_bitcast_fusion.1, f32[6,6,1,64,64]{4,3,1,0,2:T(8,128)S(1)} %copy-done.3), kind=kLoop, calls=%fused_computation.23 | loop fusion | flops 884736 | bytes 3538944 | tf_op jit(solution)/shard_map/stack | solution.py:65
  104.0 0.6 slice_select_fusion.1
  104.6 0.4 copy-done.7
  105.0 2.8 %fusion.20 = f32[4,4,3,64,64]{3,4,2,1,0:T(8,128)S(1)} fusion(f32[4,4,64,64,1]{3,2,4,1,0:T(8,128)S(1)} %copy-done.7, f32[4,4,3,64,64]{4,3,1,0,2:T(8,128)S(1)} %get-tuple-element.20), kind=kOutput, calls=%fused_computation.42 | convolution fusion | flops 150994944 | bytes 1835008 | tf_op jit(solution)/shard_map/...ij,...jk->...ik/dot_general | solution.py:29
  107.9 2.6 %fusion.17 = f32[4,4,3,64,64]{3,4,2,1,0:T(8,128)S(1)} fusion(f32[4,4,64,64,1]{3,2,4,1,0:T(8,128)S(1)} %copy-done.6, f32[4,4,3,64,64]{4,3,1,0,2:T(8,128)S(1)} %get-tuple-element.19), kind=kOutput, calls=%fused_computation.41 | convolution fusion | flops 150994944 | bytes 1835008 | tf_op jit(solution)/shard_map/...ij,...jk->...ik/dot_general | solution.py:29
  110.7 1.9 %collective-permute-start.8 = (f32[1,4,7,64,64]{3,4,2,1,0:T(8,128)S(1)}, f32[1,4,7,64,64]{3,4,2,1,0:T(8,128)S(1)}, u32[]{:S(2)}, u32[]{:S(2)}) collective-permute-start(f32[1,4,7,64,64]{3,4,2,1,0:T(8,128)S(1)} %get-tuple-element.18), channel_id=1, source_target_pairs={{16,0},{32,16},{48,32},{64,48},{80,64},{96,80},{112,96},{128,112},... | collective-permute-start | bytes 1376264 | tf_op jit(solution)/shard_map/ppermute | solution.py:21
  112.6 3.4 %collective-permute-start.9 = (f32[1,4,7,64,64]{3,4,2,1,0:T(8,128)S(1)}, f32[1,4,7,64,64]{3,4,2,1,0:T(8,128)S(1)}, u32[]{:S(2)}, u32[]{:S(2)}) collective-permute-start(f32[1,4,7,64,64]{3,4,2,1,0:T(8,128)S(1)} %get-tuple-element.17), channel_id=1, source_target_pairs={{0,16},{16,32},{32,48},{48,64},{64,80},{80,96},{96,112},{112,128},... | collective-permute-start | bytes 1376264 | tf_op jit(solution)/shard_map/ppermute | solution.py:19
  116.0 2.3 %fusion.56 = f32[4,4]{1,0:T(4,128)S(1)} fusion(f32[4,4,64,64]{3,2,1,0:T(8,128)S(1)} %copy-done.8, f32[8,8,64,64]{3,2,1,0:T(8,128)} %copy-done.5, pred[4,4]{1,0:T(4,128)(4,1)S(1)} %bitcast.106), kind=kOutput, calls=%fused_computation.93 | convolution fusion | flops 50528240 | bytes 1310800 | tf_op jit(solution)/shard_map/...ij,...kj->...ik/dot_general | solution.py:41
  118.3 0.6 copy.71
  118.9 15.8 %collective-permute-done.8 = f32[1,4,7,64,64]{3,4,2,1,0:T(8,128)S(1)} collective-permute-done((f32[1,4,7,64,64]{3,4,2,1,0:T(8,128)S(1)}, f32[1,4,7,64,64]{3,4,2,1,0:T(8,128)S(1)}, u32[]{:S(2)}, u32[]{:S(2)}) %collective-permute-start.8) | collective-permute-done | bytes 458784 | tf_op jit(solution)/shard_map/ppermute | solution.py:21
  134.7 4.0 %collective-permute-done.9 = f32[1,4,7,64,64]{3,4,2,1,0:T(8,128)S(1)} collective-permute-done((f32[1,4,7,64,64]{3,4,2,1,0:T(8,128)S(1)}, f32[1,4,7,64,64]{3,4,2,1,0:T(8,128)S(1)}, u32[]{:S(2)}, u32[]{:S(2)}) %collective-permute-start.9) | collective-permute-done | bytes 458784 | tf_op jit(solution)/shard_map/ppermute | solution.py:19
  138.8 1.9 %pad_maximum_fusion.24 = (f32[6,1,7,64,64]{3,4,2,1,0:T(8,128)}, f32[6,1,7,64,64]{3,4,2,1,0:T(8,128)}) fusion(f32[1,4,7,64,64]{3,4,2,1,0:T(8,128)S(1)} %collective-permute-done.8, f32[1,4,7,64,64]{3,4,2,1,0:T(8,128)S(1)} %collective-permute-done.9, f32[4,4,3,64,64]{3,4,2,1,0:T(8,128)S(1)} %fusion.20, f32[4,4,3,64,64]{3,4,2,1,0:T(8,128)S(1)} %fusion.17, ...), kind=kLoop, calls=%fused_computation.49 | loop fusion | flops 1376256 | bytes 4128768 | tf_op jit(solution)/shard_map/slice | solution.py:15
  140.7 3.1 %collective-permute-start.11 = (f32[6,1,7,64,64]{3,4,2,1,0:T(8,128)}, f32[6,1,7,64,64]{3,4,2,1,0:T(8,128)}, u32[]{:S(2)}, u32[]{:S(2)}) collective-permute-start(f32[6,1,7,64,64]{3,4,2,1,0:T(8,128)} %get-tuple-element.14), channel_id=1, source_target_pairs={{0,1},{1,2},{2,3},{3,4},{4,5},{5,6},{6,7},{7,8},{8,9},{9,10},{10,1... | collective-permute-start | bytes 2064392 | tf_op jit(solution)/shard_map/ppermute | solution.py:19
  143.8 1.9 %collective-permute-start.10 = (f32[6,1,7,64,64]{3,4,2,1,0:T(8,128)}, f32[6,1,7,64,64]{3,4,2,1,0:T(8,128)}, u32[]{:S(2)}, u32[]{:S(2)}) collective-permute-start(f32[6,1,7,64,64]{3,4,2,1,0:T(8,128)} %get-tuple-element.13), channel_id=1, source_target_pairs={{1,0},{2,1},{3,2},{4,3},{5,4},{6,5},{7,6},{8,7},{9,8},{10,9},{11,1... | collective-permute-start | bytes 2064392 | tf_op jit(solution)/shard_map/ppermute | solution.py:21
  145.8 2.3 %fusion.1 = f32[4,4,7,64,64]{3,4,2,1,0:T(8,128)} fusion(f32[1,4,7,64,64]{3,4,2,1,0:T(8,128)S(1)} %collective-permute-done.9, f32[4,4,3,64,64]{3,4,2,1,0:T(8,128)S(1)} %fusion.20, f32[4,4,3,64,64]{3,4,2,1,0:T(8,128)S(1)} %fusion.17, f32[4,4,1,64,64]{3,4,2,1,0:T(8,128)S(1)} %copy-done, f32[1,4,7,64,64]{3,4,2,1,0:T(8,128)S(1)} %collective-permute-done.8, ...), kind=kLoop, calls=%fused_computation.17 | loop fusion | flops 3211264 | bytes 4587536 | tf_op jit(solution)/shard_map/jit(_where)/select_n | solution.py:54
  148.1 4.3 %gather_fusion.1 = f32[12,7,64,64]{2,3,1,0:T(8,128)} fusion(f32[16,7,64,64]{2,3,1,0:T(8,128)} %bitcast.97, s32[1024]{0:T(1024)S(1)} %pad_clamp_fusion.1), kind=kCustom, calls=%fused_computation.clone | custom fusion | bytes 2752560 | tf_op jit(solution)/shard_map/jit(_take)/gather | solution.py:102
  152.4 6.0 %fusion.7 = f32[12,7,64,64]{2,3,1,0:T(8,128)} fusion(f32[12,7,64,64]{2,3,1,0:T(8,128)} %gather_fusion.1, pred[12]{0:T(512)(128)(4,1)S(1)} %compare_and_fusion, f32[12,2,64,64]{3,2,0,1:T(8,128)} %copy_select_fusion), kind=kOutput, calls=%fused_computation.33 | convolution fusion | flops 264585216 | bytes 4521996 | tf_op jit(solution)/shard_map/...ij,...jk->...ik/dot_general | solution.py:29
  158.5 3.3 %copy.69 = f32[12,7,64,64]{3,2,1,0:T(8,128)} copy(f32[12,7,64,64]{2,3,1,0:T(8,128)} %fusion.7) | data formatting | bytes 2752512 | tf_op jit(solution)/shard_map/...ij,...jk->...ik/transpose | solution.py:29
  161.8 3.2 %concatenate.101 = f32[12,7,4096]{2,1,0:T(8,128)} reshape(f32[12,7,64,64]{3,2,1,0:T(8,128)} %copy.69) | data formatting | bytes 2752512 | tf_op jit(solution)/shard_map/concatenate | solution.py:107
  165.0 3.8 %fusion = f32[4,4,7,64,64]{3,4,2,1,0:T(8,128)} fusion(f32[6,1,7,64,64]{3,4,2,1,0:T(8,128)} %collective-permute-done.11, f32[1,4,7,64,64]{3,4,2,1,0:T(8,128)} %copy-done.1, f32[1,4,7,64,64]{3,4,2,1,0:T(8,128)} %copy-done.2, f32[4,4,3,64,64]{3,4,2,1,0:T(8,128)S(1)} %fusion.20, f32[4,4,3,64,64]{3,4,2,1,0:T(8,128)S(1)} %fusion.17, f32[4,4,1,64,64]{3,4,2,1,0:T(8,128)} %copy.67, ...), kind=kLoop, calls=%fused_computation.6 | loop fusion | flops 5046272 | bytes 5963792 | tf_op jit(solution)/shard_map/jit(_where)/select_n | solution.py:55
  168.8 2.8 %gather_fusion.2 = f32[12,7,64,64]{2,3,1,0:T(8,128)S(1)} fusion(f32[16,7,64,64]{2,3,1,0:T(8,128)} %bitcast.98, s32[1024]{0:T(1024)S(1)} %pad_clamp_fusion.1), kind=kCustom, calls=%fused_computation.1.clone | custom fusion | bytes 2752560 | tf_op jit(solution)/shard_map/jit(_take)/gather | solution.py:103
  171.6 5.2 %fusion.10 = f32[12,7,64,64]{2,3,1,0:T(8,128)} fusion(f32[12,7,64,64]{2,3,1,0:T(8,128)S(1)} %gather_fusion.2, pred[12]{0:T(512)(128)(4,1)S(1)} %compare_and_fusion, f32[12,2,64,64]{3,2,0,1:T(8,128)} %copy_select_fusion), kind=kOutput, calls=%fused_computation.34 | convolution fusion | flops 264585216 | bytes 3145740 | tf_op jit(solution)/shard_map/...ij,...jk->...ik/dot_general | solution.py:29
  176.8 2.2 %copy.70 = f32[12,7,64,64]{3,2,1,0:T(8,128)S(1)} copy(f32[12,7,64,64]{2,3,1,0:T(8,128)} %fusion.10) | data formatting | bytes 2752512 | tf_op jit(solution)/shard_map/...ij,...jk->...ik/transpose | solution.py:29
  179.0 1.9 %concatenate.105 = f32[12,7,4096]{2,1,0:T(8,128)} reshape(f32[12,7,64,64]{3,2,1,0:T(8,128)S(1)} %copy.70) | data formatting | bytes 2752512 | tf_op jit(solution)/shard_map/concatenate | solution.py:107
  180.8 3.6 %fusion.2 = bf16[12,14,4096]{2,1,0:T(8,128)(2,1)} fusion(f32[12,7,4096]{2,1,0:T(8,128)} %concatenate.105, f32[12,7,4096]{2,1,0:T(8,128)} %concatenate.101, f32[12]{0:T(128)S(1)} %convert_element_type.28), kind=kLoop, calls=%fused_computation.25 | loop fusion | flops 2064384 | bytes 4128816 | tf_op jit(solution)/shard_map/convert_element_type | solution.py:110
  (72 shorter events, 2.9 us)
Async XLA Ops:
  1.9 5.5 %copy-start.11 = (s32[4,4]{1,0:T(4,128)S(1)}, s32[4,4]{1,0:T(4,128)}, u32[]{:S(2)}) copy-start(s32[4,4]{1,0:T(4,128)} %param.9) | copy-start | bytes 196
  5.6 0.8 copy-start.4
  10.0 27.0 %collective-permute-start.1 = (f32[2,4,4,64,64]{4,3,1,0,2:T(8,128)}, f32[2,4,4,64,64]{4,3,1,0,2:T(8,128)S(1)}, u32[]{:S(2)}, u32[]{:S(2)}) collective-permute-start(f32[2,4,4,64,64]{4,3,1,0,2:T(8,128)} %get-tuple-element.22), channel_id=1, source_target_pairs={{16,0},{32,16},{48,32},{64,48},{80,64},{96,80},{112,96},{128,112},... | collective-permute-start | bytes 1572872 | tf_op jit(solution)/shard_map/ppermute | solution.py:21
  15.0 28.1 %collective-permute-start = (f32[2,4,4,64,64]{4,3,1,0,2:T(8,128)}, f32[2,4,4,64,64]{4,3,1,0,2:T(8,128)}, u32[]{:S(2)}, u32[]{:S(2)}) collective-permute-start(f32[2,4,4,64,64]{4,3,1,0,2:T(8,128)} %get-tuple-element.21), channel_id=1, source_target_pairs={{0,16},{16,32},{32,48},{48,64},{64,80},{80,96},{96,112},{112,128},... | collective-permute-start | bytes 1572872 | tf_op jit(solution)/shard_map/ppermute | solution.py:19
  16.9 38.7 %collective-permute-start.5 = (s32[2,4]{1,0:T(2,128)S(1)}, s32[2,4]{1,0:T(2,128)S(1)}, u32[]{:S(2)}, u32[]{:S(2)}) collective-permute-start(s32[2,4]{1,0:T(2,128)S(1)} %get-tuple-element.30), channel_id=1, source_target_pairs={{16,0},{32,16},{48,32},{64,48},{80,64},{96,80},{112,96},{128,112},... | collective-permute-start | bytes 104 | tf_op jit(solution)/shard_map/ppermute | solution.py:21
  22.4 33.3 %collective-permute-start.4 = (s32[2,4]{1,0:T(2,128)S(1)}, s32[2,4]{1,0:T(2,128)S(1)}, u32[]{:S(2)}, u32[]{:S(2)}) collective-permute-start(s32[2,4]{1,0:T(2,128)S(1)} %get-tuple-element.29), channel_id=1, source_target_pairs={{0,16},{16,32},{32,48},{48,64},{64,80},{80,96},{96,112},{112,128},... | collective-permute-start | bytes 104 | tf_op jit(solution)/shard_map/ppermute | solution.py:19
  47.0 32.4 %collective-permute-start.3 = (f32[8,2,4,64,64]{4,3,1,0,2:T(8,128)}, f32[8,2,4,64,64]{4,3,1,0,2:T(8,128)}, u32[]{:S(2)}, u32[]{:S(2)}) collective-permute-start(f32[8,2,4,64,64]{4,3,1,0,2:T(8,128)} %get-tuple-element.16), channel_id=1, source_target_pairs={{1,0},{2,1},{3,2},{4,3},{5,4},{6,5},{7,6},{8,7},{9,8},{10,9},{11,1... | collective-permute-start | bytes 3145736 | tf_op jit(solution)/shard_map/ppermute | solution.py:21
  50.7 28.6 %collective-permute-start.2 = (f32[8,2,4,64,64]{4,3,1,0,2:T(8,128)}, f32[8,2,4,64,64]{4,3,1,0,2:T(8,128)}, u32[]{:S(2)}, u32[]{:S(2)}) collective-permute-start(f32[8,2,4,64,64]{4,3,1,0,2:T(8,128)} %get-tuple-element.15), channel_id=1, source_target_pairs={{0,1},{1,2},{2,3},{3,4},{4,5},{5,6},{6,7},{7,8},{8,9},{9,10},{10,1... | collective-permute-start | bytes 3145736 | tf_op jit(solution)/shard_map/ppermute | solution.py:19
  55.8 21.7 %collective-permute-start.7 = (s32[8,2]{1,0:T(8,128)S(1)}, s32[8,2]{1,0:T(8,128)S(1)}, u32[]{:S(2)}, u32[]{:S(2)}) collective-permute-start(s32[8,2]{1,0:T(8,128)S(1)} %get-tuple-element.26), channel_id=1, source_target_pairs={{1,0},{2,1},{3,2},{4,3},{5,4},{6,5},{7,6},{8,7},{9,8},{10,9},{11,1... | collective-permute-start | bytes 200 | tf_op jit(solution)/shard_map/ppermute | solution.py:21
  57.7 20.9 %collective-permute-start.6 = (s32[8,2]{1,0:T(8,128)S(1)}, s32[8,2]{1,0:T(8,128)S(1)}, u32[]{:S(2)}, u32[]{:S(2)}) collective-permute-start(s32[8,2]{1,0:T(8,128)S(1)} %get-tuple-element.25), channel_id=1, source_target_pairs={{0,1},{1,2},{2,3},{3,4},{4,5},{5,6},{6,7},{7,8},{8,9},{9,10},{10,1... | collective-permute-start | bytes 200 | tf_op jit(solution)/shard_map/ppermute | solution.py:19
  83.8 6.4 %copy-start.5 = (f32[8,8,64,64]{3,2,1,0:T(8,128)}, f32[8,8,64,64]{3,2,1,0:T(8,128)S(1)}, u32[]{:S(2)}) copy-start(f32[8,8,64,64]{3,2,1,0:T(8,128)S(1)} %get-tuple-element.12) | copy-start | bytes 3145732
  98.7 2.4 %copy-start.9 = (f32[4,4,1,64,64]{4,3,1,0,2:T(8,128)S(1)}, f32[4,4,1,64,64]{4,3,1,0,2:T(8,128)}, u32[]{:S(2)}) copy-start(f32[4,4,1,64,64]{4,3,1,0,2:T(8,128)} %slice_bitcast_fusion.3) | copy-start | bytes 786436
  98.7 3.4 %copy-start.3 = (f32[6,6,1,64,64]{4,3,1,0,2:T(8,128)S(1)}, f32[6,6,1,64,64]{4,3,1,0,2:T(8,128)}, u32[]{:S(2)}) copy-start(f32[6,6,1,64,64]{4,3,1,0,2:T(8,128)} %slice_bitcast_fusion.2) | copy-start | bytes 1769476
  98.7 3.4 %copy-start.10 = (f32[6,6,1,64,64]{4,3,1,0,2:T(8,128)S(1)}, f32[6,6,1,64,64]{4,3,1,0,2:T(8,128)}, u32[]{:S(2)}) copy-start(f32[6,6,1,64,64]{4,3,1,0,2:T(8,128)} %convolution_bitcast_fusion) | copy-start | bytes 1769476
  104.0 1.0 copy-start.7
  104.6 3.2 %copy-start.6 = (f32[4,4,64,64,1]{3,2,4,1,0:T(8,128)S(1)}, f32[4,4,64,64,1]{3,2,4,1,0:T(8,128)}, u32[]{:S(2)}) copy-start(f32[4,4,64,64,1]{3,2,4,1,0:T(8,128)} %convolution_bitcast_fusion.3) | copy-start | bytes 786436
  107.9 2.6 %copy-start = (f32[4,4,1,64,64]{3,4,2,1,0:T(8,128)S(1)}, f32[4,4,1,64,64]{3,4,2,1,0:T(8,128)}, u32[]{:S(2)}) copy-start(f32[4,4,1,64,64]{3,4,2,1,0:T(8,128)} %copy.67) | copy-start | bytes 786436
  110.5 5.5 %copy-start.8 = (f32[4,4,64,64]{3,2,1,0:T(8,128)S(1)}, f32[4,4,64,64]{3,2,1,0:T(8,128)}, u32[]{:S(2)}) copy-start(f32[4,4,64,64]{3,2,1,0:T(8,128)} %fusion.62) | copy-start | bytes 786436
  110.7 24.1 %collective-permute-start.8 = (f32[1,4,7,64,64]{3,4,2,1,0:T(8,128)S(1)}, f32[1,4,7,64,64]{3,4,2,1,0:T(8,128)S(1)}, u32[]{:S(2)}, u32[]{:S(2)}) collective-permute-start(f32[1,4,7,64,64]{3,4,2,1,0:T(8,128)S(1)} %get-tuple-element.18), channel_id=1, source_target_pairs={{16,0},{32,16},{48,32},{64,48},{80,64},{96,80},{112,96},{128,112},... | collective-permute-start | bytes 1376264 | tf_op jit(solution)/shard_map/ppermute | solution.py:21
  112.6 26.2 %collective-permute-start.9 = (f32[1,4,7,64,64]{3,4,2,1,0:T(8,128)S(1)}, f32[1,4,7,64,64]{3,4,2,1,0:T(8,128)S(1)}, u32[]{:S(2)}, u32[]{:S(2)}) collective-permute-start(f32[1,4,7,64,64]{3,4,2,1,0:T(8,128)S(1)} %get-tuple-element.17), channel_id=1, source_target_pairs={{0,16},{16,32},{32,48},{48,64},{64,80},{80,96},{96,112},{112,128},... | collective-permute-start | bytes 1376264 | tf_op jit(solution)/shard_map/ppermute | solution.py:19
  134.7 11.0 %copy-start.1 = (f32[1,4,7,64,64]{3,4,2,1,0:T(8,128)}, f32[1,4,7,64,64]{3,4,2,1,0:T(8,128)S(1)}, u32[]{:S(2)}) copy-start(f32[1,4,7,64,64]{3,4,2,1,0:T(8,128)S(1)} %collective-permute-done.8) | copy-start | bytes 1376260
  138.8 7.0 %copy-start.2 = (f32[1,4,7,64,64]{3,4,2,1,0:T(8,128)}, f32[1,4,7,64,64]{3,4,2,1,0:T(8,128)S(1)}, u32[]{:S(2)}) copy-start(f32[1,4,7,64,64]{3,4,2,1,0:T(8,128)S(1)} %collective-permute-done.9) | copy-start | bytes 1376260
  140.7 24.3 %collective-permute-start.11 = (f32[6,1,7,64,64]{3,4,2,1,0:T(8,128)}, f32[6,1,7,64,64]{3,4,2,1,0:T(8,128)}, u32[]{:S(2)}, u32[]{:S(2)}) collective-permute-start(f32[6,1,7,64,64]{3,4,2,1,0:T(8,128)} %get-tuple-element.14), channel_id=1, source_target_pairs={{0,1},{1,2},{2,3},{3,4},{4,5},{5,6},{6,7},{7,8},{8,9},{9,10},{10,1... | collective-permute-start | bytes 2064392 | tf_op jit(solution)/shard_map/ppermute | solution.py:19
  143.8 21.2 %collective-permute-start.10 = (f32[6,1,7,64,64]{3,4,2,1,0:T(8,128)}, f32[6,1,7,64,64]{3,4,2,1,0:T(8,128)}, u32[]{:S(2)}, u32[]{:S(2)}) collective-permute-start(f32[6,1,7,64,64]{3,4,2,1,0:T(8,128)} %get-tuple-element.13), channel_id=1, source_target_pairs={{1,0},{2,1},{3,2},{4,3},{5,4},{6,5},{7,6},{8,7},{9,8},{10,9},{11,1... | collective-permute-start | bytes 2064392 | tf_op jit(solution)/shard_map/ppermute | solution.py:21
where the time goes:
time: 186 us; the launch traced here: 184 us
  waiting for transfers between devices  46.6 us (25%)
  starting transfers between devices  39.7 us (21%)
  local copies, waits for them, and re-layouts  37.7 us (20%)
  matrix products  35.9 us (19%)
  other arithmetic  23.5 us (13%)
    ppermute x6, waiting for transfers between devices, extended(): lax.ppermute(head, axis, [((i + 1) % count, i) for i in range(ends)])  35.5 us
    dot_general x12, matrix products, matmul(): jnp.einsum('...ij,...jk->...ik', left_block, right_block, precision=lax.P...  31.4 us
    ppermute x6, starting transfers between devices, extended(): lax.ppermute(head, axis, [((i + 1) % count, i) for i in range(ends)])  19.8 us
    ppermute x6, starting transfers between devices, extended(): lax.ppermute(tail, axis, [(i, (i + 1) % count) for i in range(ends)])  19.8 us
    ppermute x6, waiting for transfers between devices, extended(): lax.ppermute(tail, axis, [(i, (i + 1) % count) for i in range(ends)])  11.1 us
    transpose x2, local copies, waits for them, and re-layouts, matmul(): jnp.einsum('...ij,...jk->...ik', left_block, right_block, precision=lax.P...  5.54 us
    concatenate x2, local copies, waits for them, and re-layouts, restriction_rows(): jnp.concatenate([matmul(coupling_rows[:, 0:1], rows_x), matmul(coupling_r...  5.03 us
    concatenate x3, other arithmetic, extended(): jnp.concatenate([lax.ppermute(tail, axis, [(i, (i + 1) % count) for i in...  4.91 us
  transfers between devices with their start and end apart: 12, of which 6 were waited for; matrix products, arithmetic and copies ran while one was open for 19% of the time, Pallas kernels for 0%

commit v1 on v0

--- a/solution.py
+++ b/solution.py
@@ -27,19 +27,19 @@
 
 def matmul(left_block, right_block):
     return jnp.einsum(
-        "...ij,...jk->...ik", left_block, right_block, precision=lax.Precision.HIGHEST
+        "...ij,...jk->...ik", left_block, right_block, precision=lax.Precision.HIGH
     )
 
 
 def left_gram(left_block, right_block):
     return jnp.einsum(
-        "...ji,...jk->...ik", left_block, right_block, precision=lax.Precision.HIGHEST
+        "...ji,...jk->...ik", left_block, right_block, precision=lax.Precision.HIGH
     )
 
 
 def right_gram(left_block, right_block):
     return jnp.einsum(
-        "...ij,...kj->...ik", left_block, right_block, precision=lax.Precision.HIGHEST
+        "...ij,...kj->...ik", left_block, right_block, precision=lax.Precision.HIGH
     )
 
 

time: 186 us -> 177 us (0.952)
  matrix products: 35.9 us -> 25.9 us
    dot_general x12, matrix products: 31.4 us -> 22.7 us  [matmul(): jnp.einsum('...ij,...jk->...ik', left_block, right_block, precision=lax.P...]
  transfers between devices with their start and end apart: 12 -> 12, of which waited for: 6 -> 7; matrix products, arithmetic and copies ran while one was open for 19% -> 19% of each run, Pallas kernels for 0% -> 0%
where the time goes in v1:
time: 177 us; the launch traced here: 176 us
  waiting for transfers between devices  48 us (27%)
  starting transfers between devices  40.1 us (23%)
  local copies, waits for them, and re-layouts  37.7 us (21%)
  matrix products  25.9 us (15%)
  other arithmetic  23.3 us (13%)
    ppermute x6, waiting for transfers between devices, extended(): lax.ppermute(head, axis, [((i + 1) % count, i) for i in range(ends)])  36.9 us
    dot_general x12, matrix products, matmul(): jnp.einsum('...ij,...jk->...ik', left_block, right_block, precision=lax.P...  22.7 us
    ppermute x6, starting transfers between devices, extended(): lax.ppermute(head, axis, [((i + 1) % count, i) for i in range(ends)])  20.1 us
    ppermute x6, starting transfers between devices, extended(): lax.ppermute(tail, axis, [(i, (i + 1) % count) for i in range(ends)])  20 us
    ppermute x6, waiting for transfers between devices, extended(): lax.ppermute(tail, axis, [(i, (i + 1) % count) for i in range(ends)])  11.1 us
    transpose x2, local copies, waits for them, and re-layouts, matmul(): jnp.einsum('...ij,...jk->...ik', left_block, right_block, precision=lax.P...  5.54 us
    concatenate x2, local copies, waits for them, and re-layouts, restriction_rows(): jnp.concatenate([matmul(coupling_rows[:, 0:1], rows_x), matmul(coupling_r...  5.03 us
    concatenate x3, other arithmetic, extended(): jnp.concatenate([lax.ppermute(tail, axis, [(i, (i + 1) % count) for i in...  4.73 us
  transfers between devices with their start and end apart: 12, of which 7 were waited for; matrix products, arithmetic and copies ran while one was open for 19% of the time, Pallas kernels for 0%

profile of v1, /device:TPU:103, one launch (start us, length us, event | category | flops | bytes accessed | tf_op | source)
XLA Modules:
  0.0 175.9 jit_solution(10318568839281343445)
XLA Ops:
  0.6 1.2 reshape.516
  1.9 1.3 broadcast_in_dim_reshape.4
  3.1 0.8 fusion.77
  4.3 1.3 broadcast_multiply_fusion
  5.6 0.8 copy-done.4
  6.8 0.5 reshape.517
  7.4 0.6 fusion.27
  8.2 1.5 fusion.75
  9.6 4.9 %collective-permute-start.1 = (f32[2,4,4,64,64]{4,3,1,0,2:T(8,128)}, f32[2,4,4,64,64]{4,3,1,0,2:T(8,128)S(1)}, u32[]{:S(2)}, u32[]{:S(2)}) collective-permute-start(f32[2,4,4,64,64]{4,3,1,0,2:T(8,128)} %get-tuple-element.22), channel_id=1, source_target_pairs={{16,0},{32,16},{48,32},{64,48},{80,64},{96,80},{112,96},{128,112},... | collective-permute-start | bytes 1572872 | tf_op jit(solution)/shard_map/ppermute | solution.py:21
  14.5 1.9 %collective-permute-start = (f32[2,4,4,64,64]{4,3,1,0,2:T(8,128)}, f32[2,4,4,64,64]{4,3,1,0,2:T(8,128)}, u32[]{:S(2)}, u32[]{:S(2)}) collective-permute-start(f32[2,4,4,64,64]{4,3,1,0,2:T(8,128)} %get-tuple-element.21), channel_id=1, source_target_pairs={{0,16},{16,32},{32,48},{48,64},{64,80},{80,96},{96,112},{112,128},... | collective-permute-start | bytes 1572872 | tf_op jit(solution)/shard_map/ppermute | solution.py:19
  16.5 5.5 %collective-permute-start.5 = (s32[2,4]{1,0:T(2,128)S(1)}, s32[2,4]{1,0:T(2,128)S(1)}, u32[]{:S(2)}, u32[]{:S(2)}) collective-permute-start(s32[2,4]{1,0:T(2,128)S(1)} %get-tuple-element.30), channel_id=1, source_target_pairs={{16,0},{32,16},{48,32},{64,48},{80,64},{96,80},{112,96},{128,112},... | collective-permute-start | bytes 104 | tf_op jit(solution)/shard_map/ppermute | solution.py:21
  22.0 1.9 %collective-permute-start.4 = (s32[2,4]{1,0:T(2,128)S(1)}, s32[2,4]{1,0:T(2,128)S(1)}, u32[]{:S(2)}, u32[]{:S(2)}) collective-permute-start(s32[2,4]{1,0:T(2,128)S(1)} %get-tuple-element.29), channel_id=1, source_target_pairs={{0,16},{16,32},{32,48},{48,64},{64,80},{80,96},{96,112},{112,128},... | collective-permute-start | bytes 104 | tf_op jit(solution)/shard_map/ppermute | solution.py:19
  24.4 2.6 %reshape_reshape.3 = f32[16,2,64,64]{3,2,1,0:T(8,128)} reshape(f32[4,4,2,4096]{3,2,1,0:T(2,128)} %copy-done.4) | data formatting | bytes 1048576 | tf_op jit(solution)/shard_map/reshape;reshape | solution.py:105
  27.0 2.7 %gather_fusion = f32[12,2,64,64]{3,2,1,0:T(8,128)} fusion(f32[16,2,64,64]{3,2,1,0:T(8,128)} %reshape_reshape.3, s32[1024]{0:T(1024)S(1)} %pad_clamp_fusion), kind=kCustom, calls=%fused_computation.2 | custom fusion | bytes 786480 | tf_op jit(solution)/shard_map/jit(_take)/gather | solution.py:104
  29.7 2.1 %copy_select_fusion = f32[12,2,64,64]{3,2,0,1:T(8,128)} fusion(f32[12,2,64,64]{3,2,1,0:T(8,128)} %gather_fusion, pred[12]{0:T(512)(128)(4,1)S(1)} %compare_and_fusion), kind=kLoop, calls=%fused_computation.98 | loop fusion | flops 98304 | bytes 786444 | tf_op jit(solution)/shard_map/jit(_take)/select_n | solution.py:104
  31.8 4.8 %collective-permute-done.1 = f32[2,4,4,64,64]{4,3,1,0,2:T(8,128)S(1)} collective-permute-done((f32[2,4,4,64,64]{4,3,1,0,2:T(8,128)}, f32[2,4,4,64,64]{4,3,1,0,2:T(8,128)S(1)}, u32[]{:S(2)}, u32[]{:S(2)}) %collective-permute-start.1) | collective-permute-done | bytes 524320 | tf_op jit(solution)/shard_map/ppermute | solution.py:21
  36.7 5.9 %collective-permute-done = f32[2,4,4,64,64]{4,3,1,0,2:T(8,128)} collective-permute-done((f32[2,4,4,64,64]{4,3,1,0,2:T(8,128)}, f32[2,4,4,64,64]{4,3,1,0,2:T(8,128)}, u32[]{:S(2)}, u32[]{:S(2)}) %collective-permute-start) | collective-permute-done | bytes 524320 | tf_op jit(solution)/shard_map/ppermute | solution.py:19
  42.6 1.7 pad_maximum_fusion.1
  44.3 2.3 %fusion.74 = (f32[8,2,4,64,64]{4,3,1,0,2:T(8,128)}, f32[8,2,4,64,64]{4,3,1,0,2:T(8,128)}) fusion(f32[8,4,4,64,64]{4,3,1,0,2:T(8,128)S(1)} %pad_maximum_fusion.1), kind=kLoop, calls=%fused_computation.163 | loop fusion | bytes 4194304 | tf_op jit(solution)/shard_map/slice | solution.py:16
  46.6 3.7 %collective-permute-start.3 = (f32[8,2,4,64,64]{4,3,1,0,2:T(8,128)}, f32[8,2,4,64,64]{4,3,1,0,2:T(8,128)}, u32[]{:S(2)}, u32[]{:S(2)}) collective-permute-start(f32[8,2,4,64,64]{4,3,1,0,2:T(8,128)} %get-tuple-element.16), channel_id=1, source_target_pairs={{1,0},{2,1},{3,2},{4,3},{5,4},{6,5},{7,6},{8,7},{9,8},{10,9},{11,1... | collective-permute-start | bytes 3145736 | tf_op jit(solution)/shard_map/ppermute | solution.py:21
  50.3 4.7 %collective-permute-start.2 = (f32[8,2,4,64,64]{4,3,1,0,2:T(8,128)}, f32[8,2,4,64,64]{4,3,1,0,2:T(8,128)}, u32[]{:S(2)}, u32[]{:S(2)}) collective-permute-start(f32[8,2,4,64,64]{4,3,1,0,2:T(8,128)} %get-tuple-element.15), channel_id=1, source_target_pairs={{0,1},{1,2},{2,3},{3,4},{4,5},{5,6},{6,7},{7,8},{8,9},{9,10},{10,1... | collective-permute-start | bytes 3145736 | tf_op jit(solution)/shard_map/ppermute | solution.py:19
  55.4 1.9 %collective-permute-start.7 = (s32[8,2]{1,0:T(8,128)S(1)}, s32[8,2]{1,0:T(8,128)S(1)}, u32[]{:S(2)}, u32[]{:S(2)}) collective-permute-start(s32[8,2]{1,0:T(8,128)S(1)} %get-tuple-element.26), channel_id=1, source_target_pairs={{1,0},{2,1},{3,2},{4,3},{5,4},{6,5},{7,6},{8,7},{9,8},{10,9},{11,1... | collective-permute-start | bytes 200 | tf_op jit(solution)/shard_map/ppermute | solution.py:21
  57.3 5.0 %collective-permute-start.6 = (s32[8,2]{1,0:T(8,128)S(1)}, s32[8,2]{1,0:T(8,128)S(1)}, u32[]{:S(2)}, u32[]{:S(2)}) collective-permute-start(s32[8,2]{1,0:T(8,128)S(1)} %get-tuple-element.25), channel_id=1, source_target_pairs={{0,1},{1,2},{2,3},{3,4},{4,5},{5,6},{6,7},{7,8},{8,9},{9,10},{10,1... | collective-permute-start | bytes 200 | tf_op jit(solution)/shard_map/ppermute | solution.py:19
  62.4 14.7 %collective-permute-done.7 = s32[8,2]{1,0:T(8,128)S(1)} collective-permute-done((s32[8,2]{1,0:T(8,128)S(1)}, s32[8,2]{1,0:T(8,128)S(1)}, u32[]{:S(2)}, u32[]{:S(2)}) %collective-permute-start.7) | collective-permute-done | bytes 96 | tf_op jit(solution)/shard_map/ppermute | solution.py:21
  77.1 1.1 collective-permute-done.6
  79.0 3.1 %pad_maximum_fusion = f32[8,8,4,64,64]{4,3,1,0,2:T(8,128)S(1)} fusion(f32[8,2,4,64,64]{4,3,1,0,2:T(8,128)} %collective-permute-done.3, f32[2,4,4,64,64]{4,3,1,0,2:T(8,128)S(1)} %collective-permute-done.1, f32[4,4,2,64,64]{4,3,1,0,2:T(8,128)S(1)} %reshape.517, f32[4,4,1,64,64]{4,3,1,0,2:T(8,128)S(1)} %fusion.27, ...), kind=kLoop, calls=%fused_computation.3 | loop fusion | flops 6291456 | bytes 8388608 | tf_op jit(solution)/shard_map/concatenate | solution.py:17
  82.4 0.5 slice_bitcast_fusion
  82.9 1.5 fusion.62
  84.4 1.2 convolution_bitcast_fusion.2
  85.6 1.2 convolution_bitcast_fusion.3
  86.8 1.1 slice_bitcast_fusion.2
  87.9 0.8 slice_bitcast_fusion.3
  88.7 0.7 fusion.57
  89.4 1.9 %fusion.28 = f32[6,6,64,64]{3,2,1,0:T(8,128)S(1)} fusion(f32[8,8,64,64]{3,2,1,0:T(8,128)S(1)} %get-tuple-element.11, f32[8,2,4,64,64]{4,3,1,0,2:T(8,128)} %collective-permute-done.3, f32[8,2,4,64,64]{4,3,1,0,2:T(8,128)} %collective-permute-done.2, f32[2,4,4,64,64]{4,3,1,0,2:T(8,128)S(1)} %collective-permute-done.1, ...), kind=kOutput, calls=%fused_computation.61 | convolution fusion | flops 57655296 | bytes 8717312 | tf_op jit(solution)/shard_map/...ij,...jk->...ik/dot_general | solution.py:29
  91.3 1.7 convolution_bitcast_fusion
  93.0 1.9 %fusion.42 = f32[6,6,64,64]{3,2,1,0:T(8,128)S(1)} fusion(f32[8,8,64,64]{3,2,1,0:T(8,128)S(1)} %get-tuple-element.11, f32[8,2,4,64,64]{4,3,1,0,2:T(8,128)} %collective-permute-done.3, f32[8,2,4,64,64]{4,3,1,0,2:T(8,128)} %collective-permute-done.2, f32[2,4,4,64,64]{4,3,1,0,2:T(8,128)S(1)} %collective-permute-done.1, ...), kind=kOutput, calls=%fused_computation.77 | convolution fusion | flops 57655296 | bytes 8717312 | tf_op jit(solution)/shard_map/...ij,...jk->...ik/dot_general | solution.py:29
  94.9 1.7 convolution_bitcast_fusion.1
  96.6 1.0 copy.67
  97.6 1.9 %pad_maximum_fusion.18 = f32[6,6,3,64,64]{4,3,1,0,2:T(8,128)S(1)} fusion(f32[6,6,1,64,64]{4,3,1,0,2:T(8,128)S(1)} %copy-done.10, f32[6,6,1,64,64]{4,3,1,0,2:T(8,128)} %convolution_bitcast_fusion.1, f32[6,6,1,64,64]{4,3,1,0,2:T(8,128)S(1)} %copy-done.3), kind=kLoop, calls=%fused_computation.23 | loop fusion | flops 884736 | bytes 3538944 | tf_op jit(solution)/shard_map/stack | solution.py:65
  99.5 0.6 slice_select_fusion.1
  100.2 0.4 copy-done.7
  100.5 1.4 fusion.20
  102.0 1.4 fusion.17
  103.5 1.9 %collective-permute-start.8 = (f32[1,4,7,64,64]{3,4,2,1,0:T(8,128)S(1)}, f32[1,4,7,64,64]{3,4,2,1,0:T(8,128)S(1)}, u32[]{:S(2)}, u32[]{:S(2)}) collective-permute-start(f32[1,4,7,64,64]{3,4,2,1,0:T(8,128)S(1)} %get-tuple-element.18), channel_id=1, source_target_pairs={{16,0},{32,16},{48,32},{64,48},{80,64},{96,80},{112,96},{128,112},... | collective-permute-start | bytes 1376264 | tf_op jit(solution)/shard_map/ppermute | solution.py:21
  105.5 3.4 %collective-permute-start.9 = (f32[1,4,7,64,64]{3,4,2,1,0:T(8,128)S(1)}, f32[1,4,7,64,64]{3,4,2,1,0:T(8,128)S(1)}, u32[]{:S(2)}, u32[]{:S(2)}) collective-permute-start(f32[1,4,7,64,64]{3,4,2,1,0:T(8,128)S(1)} %get-tuple-element.17), channel_id=1, source_target_pairs={{0,16},{16,32},{32,48},{48,64},{64,80},{80,96},{96,112},{112,128},... | collective-permute-start | bytes 1376264 | tf_op jit(solution)/shard_map/ppermute | solution.py:19
  108.8 1.9 %fusion.56 = f32[4,4]{1,0:T(4,128)S(1)} fusion(f32[4,4,64,64]{3,2,1,0:T(8,128)S(1)} %copy-done.8, f32[8,8,64,64]{3,2,1,0:T(8,128)} %copy-done.5, pred[4,4]{1,0:T(4,128)(4,1)S(1)} %bitcast.106), kind=kOutput, calls=%fused_computation.93 | convolution fusion | flops 25362416 | bytes 1310800 | tf_op jit(solution)/shard_map/...ij,...kj->...ik/dot_general | solution.py:41
  110.8 0.6 copy.71
  111.4 16.2 %collective-permute-done.8 = f32[1,4,7,64,64]{3,4,2,1,0:T(8,128)S(1)} collective-permute-done((f32[1,4,7,64,64]{3,4,2,1,0:T(8,128)S(1)}, f32[1,4,7,64,64]{3,4,2,1,0:T(8,128)S(1)}, u32[]{:S(2)}, u32[]{:S(2)}) %collective-permute-start.8) | collective-permute-done | bytes 458784 | tf_op jit(solution)/shard_map/ppermute | solution.py:21
  127.6 4.0 %collective-permute-done.9 = f32[1,4,7,64,64]{3,4,2,1,0:T(8,128)S(1)} collective-permute-done((f32[1,4,7,64,64]{3,4,2,1,0:T(8,128)S(1)}, f32[1,4,7,64,64]{3,4,2,1,0:T(8,128)S(1)}, u32[]{:S(2)}, u32[]{:S(2)}) %collective-permute-start.9) | collective-permute-done | bytes 458784 | tf_op jit(solution)/shard_map/ppermute | solution.py:19
  131.6 1.9 %pad_maximum_fusion.24 = (f32[6,1,7,64,64]{3,4,2,1,0:T(8,128)}, f32[6,1,7,64,64]{3,4,2,1,0:T(8,128)}) fusion(f32[1,4,7,64,64]{3,4,2,1,0:T(8,128)S(1)} %collective-permute-done.8, f32[1,4,7,64,64]{3,4,2,1,0:T(8,128)S(1)} %collective-permute-done.9, f32[4,4,3,64,64]{3,4,2,1,0:T(8,128)S(1)} %fusion.20, f32[4,4,3,64,64]{3,4,2,1,0:T(8,128)S(1)} %fusion.17, ...), kind=kLoop, calls=%fused_computation.49 | loop fusion | flops 1376256 | bytes 4128768 | tf_op jit(solution)/shard_map/slice | solution.py:15
  133.6 3.1 %collective-permute-start.11 = (f32[6,1,7,64,64]{3,4,2,1,0:T(8,128)}, f32[6,1,7,64,64]{3,4,2,1,0:T(8,128)}, u32[]{:S(2)}, u32[]{:S(2)}) collective-permute-start(f32[6,1,7,64,64]{3,4,2,1,0:T(8,128)} %get-tuple-element.14), channel_id=1, source_target_pairs={{0,1},{1,2},{2,3},{3,4},{4,5},{5,6},{6,7},{7,8},{8,9},{9,10},{10,1... | collective-permute-start | bytes 2064392 | tf_op jit(solution)/shard_map/ppermute | solution.py:19
  136.7 2.1 %collective-permute-start.10 = (f32[6,1,7,64,64]{3,4,2,1,0:T(8,128)}, f32[6,1,7,64,64]{3,4,2,1,0:T(8,128)}, u32[]{:S(2)}, u32[]{:S(2)}) collective-permute-start(f32[6,1,7,64,64]{3,4,2,1,0:T(8,128)} %get-tuple-element.13), channel_id=1, source_target_pairs={{1,0},{2,1},{3,2},{4,3},{5,4},{6,5},{7,6},{8,7},{9,8},{10,9},{11,1... | collective-permute-start | bytes 2064392 | tf_op jit(solution)/shard_map/ppermute | solution.py:21
  138.9 2.3 %fusion.1 = f32[4,4,7,64,64]{3,4,2,1,0:T(8,128)} fusion(f32[1,4,7,64,64]{3,4,2,1,0:T(8,128)S(1)} %collective-permute-done.9, f32[4,4,3,64,64]{3,4,2,1,0:T(8,128)S(1)} %fusion.20, f32[4,4,3,64,64]{3,4,2,1,0:T(8,128)S(1)} %fusion.17, f32[4,4,1,64,64]{3,4,2,1,0:T(8,128)S(1)} %copy-done, f32[1,4,7,64,64]{3,4,2,1,0:T(8,128)S(1)} %collective-permute-done.8, ...), kind=kLoop, calls=%fused_computation.17 | loop fusion | flops 3211264 | bytes 4587536 | tf_op jit(solution)/shard_map/jit(_where)/select_n | solution.py:54
  141.2 4.3 %gather_fusion.1 = f32[12,7,64,64]{2,3,1,0:T(8,128)} fusion(f32[16,7,64,64]{2,3,1,0:T(8,128)} %bitcast.97, s32[1024]{0:T(1024)S(1)} %pad_clamp_fusion.1), kind=kCustom, calls=%fused_computation.clone | custom fusion | bytes 2752560 | tf_op jit(solution)/shard_map/jit(_take)/gather | solution.py:102
  145.5 4.7 %fusion.7 = f32[12,7,64,64]{2,3,1,0:T(8,128)} fusion(f32[12,7,64,64]{2,3,1,0:T(8,128)} %gather_fusion.1, pred[12]{0:T(512)(128)(4,1)S(1)} %compare_and_fusion, f32[12,2,64,64]{3,2,0,1:T(8,128)} %copy_select_fusion), kind=kOutput, calls=%fused_computation.33 | convolution fusion | flops 132464640 | bytes 4521996 | tf_op jit(solution)/shard_map/...ij,...jk->...ik/dot_general | solution.py:29
  150.2 3.3 %copy.69 = f32[12,7,64,64]{3,2,1,0:T(8,128)} copy(f32[12,7,64,64]{2,3,1,0:T(8,128)} %fusion.7) | data formatting | bytes 2752512 | tf_op jit(solution)/shard_map/...ij,...jk->...ik/transpose | solution.py:29
  153.6 3.2 %concatenate.101 = f32[12,7,4096]{2,1,0:T(8,128)} reshape(f32[12,7,64,64]{3,2,1,0:T(8,128)} %copy.69) | data formatting | bytes 2752512 | tf_op jit(solution)/shard_map/concatenate | solution.py:107
  156.8 1.1 collective-permute-done.10
  157.9 3.8 %fusion = f32[4,4,7,64,64]{3,4,2,1,0:T(8,128)} fusion(f32[6,1,7,64,64]{3,4,2,1,0:T(8,128)} %collective-permute-done.11, f32[1,4,7,64,64]{3,4,2,1,0:T(8,128)} %copy-done.1, f32[1,4,7,64,64]{3,4,2,1,0:T(8,128)} %copy-done.2, f32[4,4,3,64,64]{3,4,2,1,0:T(8,128)S(1)} %fusion.20, f32[4,4,3,64,64]{3,4,2,1,0:T(8,128)S(1)} %fusion.17, f32[4,4,1,64,64]{3,4,2,1,0:T(8,128)} %copy.67, ...), kind=kLoop, calls=%fused_computation.6 | loop fusion | flops 5046272 | bytes 5963792 | tf_op jit(solution)/shard_map/jit(_where)/select_n | solution.py:55
  161.7 2.8 %gather_fusion.2 = f32[12,7,64,64]{2,3,1,0:T(8,128)S(1)} fusion(f32[16,7,64,64]{2,3,1,0:T(8,128)} %bitcast.98, s32[1024]{0:T(1024)S(1)} %pad_clamp_fusion.1), kind=kCustom, calls=%fused_computation.1.clone | custom fusion | bytes 2752560 | tf_op jit(solution)/shard_map/jit(_take)/gather | solution.py:103
  164.4 3.9 %fusion.10 = f32[12,7,64,64]{2,3,1,0:T(8,128)} fusion(f32[12,7,64,64]{2,3,1,0:T(8,128)S(1)} %gather_fusion.2, pred[12]{0:T(512)(128)(4,1)S(1)} %compare_and_fusion, f32[12,2,64,64]{3,2,0,1:T(8,128)} %copy_select_fusion), kind=kOutput, calls=%fused_computation.34 | convolution fusion | flops 132464640 | bytes 3145740 | tf_op jit(solution)/shard_map/...ij,...jk->...ik/dot_general | solution.py:29
  168.3 2.2 %copy.70 = f32[12,7,64,64]{3,2,1,0:T(8,128)S(1)} copy(f32[12,7,64,64]{2,3,1,0:T(8,128)} %fusion.10) | data formatting | bytes 2752512 | tf_op jit(solution)/shard_map/...ij,...jk->...ik/transpose | solution.py:29
  170.5 1.9 %concatenate.105 = f32[12,7,4096]{2,1,0:T(8,128)} reshape(f32[12,7,64,64]{3,2,1,0:T(8,128)S(1)} %copy.70) | data formatting | bytes 2752512 | tf_op jit(solution)/shard_map/concatenate | solution.py:107
  172.4 3.6 %fusion.2 = bf16[12,14,4096]{2,1,0:T(8,128)(2,1)} fusion(f32[12,7,4096]{2,1,0:T(8,128)} %concatenate.105, f32[12,7,4096]{2,1,0:T(8,128)} %concatenate.101, f32[12]{0:T(128)S(1)} %convert_element_type.28), kind=kLoop, calls=%fused_computation.25 | loop fusion | flops 2064384 | bytes 4128816 | tf_op jit(solution)/shard_map/convert_element_type | solution.py:110
  (72 shorter events, 3.2 us)
Async XLA Ops:
  1.9 5.5 %copy-start.11 = (s32[4,4]{1,0:T(4,128)S(1)}, s32[4,4]{1,0:T(4,128)}, u32[]{:S(2)}) copy-start(s32[4,4]{1,0:T(4,128)} %param.9) | copy-start | bytes 196
  5.6 0.8 copy-start.4
  9.6 27.0 %collective-permute-start.1 = (f32[2,4,4,64,64]{4,3,1,0,2:T(8,128)}, f32[2,4,4,64,64]{4,3,1,0,2:T(8,128)S(1)}, u32[]{:S(2)}, u32[]{:S(2)}) collective-permute-start(f32[2,4,4,64,64]{4,3,1,0,2:T(8,128)} %get-tuple-element.22), channel_id=1, source_target_pairs={{16,0},{32,16},{48,32},{64,48},{80,64},{96,80},{112,96},{128,112},... | collective-permute-start | bytes 1572872 | tf_op jit(solution)/shard_map/ppermute | solution.py:21
  14.5 28.1 %collective-permute-start = (f32[2,4,4,64,64]{4,3,1,0,2:T(8,128)}, f32[2,4,4,64,64]{4,3,1,0,2:T(8,128)}, u32[]{:S(2)}, u32[]{:S(2)}) collective-permute-start(f32[2,4,4,64,64]{4,3,1,0,2:T(8,128)} %get-tuple-element.21), channel_id=1, source_target_pairs={{0,16},{16,32},{32,48},{48,64},{64,80},{80,96},{96,112},{112,128},... | collective-permute-start | bytes 1572872 | tf_op jit(solution)/shard_map/ppermute | solution.py:19
  16.5 38.7 %collective-permute-start.5 = (s32[2,4]{1,0:T(2,128)S(1)}, s32[2,4]{1,0:T(2,128)S(1)}, u32[]{:S(2)}, u32[]{:S(2)}) collective-permute-start(s32[2,4]{1,0:T(2,128)S(1)} %get-tuple-element.30), channel_id=1, source_target_pairs={{16,0},{32,16},{48,32},{64,48},{80,64},{96,80},{112,96},{128,112},... | collective-permute-start | bytes 104 | tf_op jit(solution)/shard_map/ppermute | solution.py:21
  22.0 33.3 %collective-permute-start.4 = (s32[2,4]{1,0:T(2,128)S(1)}, s32[2,4]{1,0:T(2,128)S(1)}, u32[]{:S(2)}, u32[]{:S(2)}) collective-permute-start(s32[2,4]{1,0:T(2,128)S(1)} %get-tuple-element.29), channel_id=1, source_target_pairs={{0,16},{16,32},{32,48},{48,64},{64,80},{80,96},{96,112},{112,128},... | collective-permute-start | bytes 104 | tf_op jit(solution)/shard_map/ppermute | solution.py:19
  46.6 32.4 %collective-permute-start.3 = (f32[8,2,4,64,64]{4,3,1,0,2:T(8,128)}, f32[8,2,4,64,64]{4,3,1,0,2:T(8,128)}, u32[]{:S(2)}, u32[]{:S(2)}) collective-permute-start(f32[8,2,4,64,64]{4,3,1,0,2:T(8,128)} %get-tuple-element.16), channel_id=1, source_target_pairs={{1,0},{2,1},{3,2},{4,3},{5,4},{6,5},{7,6},{8,7},{9,8},{10,9},{11,1... | collective-permute-start | bytes 3145736 | tf_op jit(solution)/shard_map/ppermute | solution.py:21
  50.3 28.6 %collective-permute-start.2 = (f32[8,2,4,64,64]{4,3,1,0,2:T(8,128)}, f32[8,2,4,64,64]{4,3,1,0,2:T(8,128)}, u32[]{:S(2)}, u32[]{:S(2)}) collective-permute-start(f32[8,2,4,64,64]{4,3,1,0,2:T(8,128)} %get-tuple-element.15), channel_id=1, source_target_pairs={{0,1},{1,2},{2,3},{3,4},{4,5},{5,6},{6,7},{7,8},{8,9},{9,10},{10,1... | collective-permute-start | bytes 3145736 | tf_op jit(solution)/shard_map/ppermute | solution.py:19
  55.4 21.7 %collective-permute-start.7 = (s32[8,2]{1,0:T(8,128)S(1)}, s32[8,2]{1,0:T(8,128)S(1)}, u32[]{:S(2)}, u32[]{:S(2)}) collective-permute-start(s32[8,2]{1,0:T(8,128)S(1)} %get-tuple-element.26), channel_id=1, source_target_pairs={{1,0},{2,1},{3,2},{4,3},{5,4},{6,5},{7,6},{8,7},{9,8},{10,9},{11,1... | collective-permute-start | bytes 200 | tf_op jit(solution)/shard_map/ppermute | solution.py:21
  57.3 20.9 %collective-permute-start.6 = (s32[8,2]{1,0:T(8,128)S(1)}, s32[8,2]{1,0:T(8,128)S(1)}, u32[]{:S(2)}, u32[]{:S(2)}) collective-permute-start(s32[8,2]{1,0:T(8,128)S(1)} %get-tuple-element.25), channel_id=1, source_target_pairs={{0,1},{1,2},{2,3},{3,4},{4,5},{5,6},{6,7},{7,8},{8,9},{9,10},{10,1... | collective-permute-start | bytes 200 | tf_op jit(solution)/shard_map/ppermute | solution.py:19
  82.9 5.8 %copy-start.5 = (f32[8,8,64,64]{3,2,1,0:T(8,128)}, f32[8,8,64,64]{3,2,1,0:T(8,128)S(1)}, u32[]{:S(2)}) copy-start(f32[8,8,64,64]{3,2,1,0:T(8,128)S(1)} %get-tuple-element.12) | copy-start | bytes 3145732
  94.8 1.7 copy-start.9
  94.9 2.7 %copy-start.3 = (f32[6,6,1,64,64]{4,3,1,0,2:T(8,128)S(1)}, f32[6,6,1,64,64]{4,3,1,0,2:T(8,128)}, u32[]{:S(2)}) copy-start(f32[6,6,1,64,64]{4,3,1,0,2:T(8,128)} %slice_bitcast_fusion.2) | copy-start | bytes 1769476
  94.9 2.7 %copy-start.10 = (f32[6,6,1,64,64]{4,3,1,0,2:T(8,128)S(1)}, f32[6,6,1,64,64]{4,3,1,0,2:T(8,128)}, u32[]{:S(2)}) copy-start(f32[6,6,1,64,64]{4,3,1,0,2:T(8,128)} %convolution_bitcast_fusion) | copy-start | bytes 1769476
  99.5 1.0 copy-start.7
  100.2 1.8 %copy-start.6 = (f32[4,4,64,64,1]{3,2,4,1,0:T(8,128)S(1)}, f32[4,4,64,64,1]{3,2,4,1,0:T(8,128)}, u32[]{:S(2)}) copy-start(f32[4,4,64,64,1]{3,2,4,1,0:T(8,128)} %convolution_bitcast_fusion.3) | copy-start | bytes 786436
  102.0 1.4 copy-start
  103.4 5.5 %copy-start.8 = (f32[4,4,64,64]{3,2,1,0:T(8,128)S(1)}, f32[4,4,64,64]{3,2,1,0:T(8,128)}, u32[]{:S(2)}) copy-start(f32[4,4,64,64]{3,2,1,0:T(8,128)} %fusion.62) | copy-start | bytes 786436
  103.5 24.1 %collective-permute-start.8 = (f32[1,4,7,64,64]{3,4,2,1,0:T(8,128)S(1)}, f32[1,4,7,64,64]{3,4,2,1,0:T(8,128)S(1)}, u32[]{:S(2)}, u32[]{:S(2)}) collective-permute-start(f32[1,4,7,64,64]{3,4,2,1,0:T(8,128)S(1)} %get-tuple-element.18), channel_id=1, source_target_pairs={{16,0},{32,16},{48,32},{64,48},{80,64},{96,80},{112,96},{128,112},... | collective-permute-start | bytes 1376264 | tf_op jit(solution)/shard_map/ppermute | solution.py:21
  105.5 26.2 %collective-permute-start.9 = (f32[1,4,7,64,64]{3,4,2,1,0:T(8,128)S(1)}, f32[1,4,7,64,64]{3,4,2,1,0:T(8,128)S(1)}, u32[]{:S(2)}, u32[]{:S(2)}) collective-permute-start(f32[1,4,7,64,64]{3,4,2,1,0:T(8,128)S(1)} %get-tuple-element.17), channel_id=1, source_target_pairs={{0,16},{16,32},{32,48},{48,64},{64,80},{80,96},{96,112},{112,128},... | collective-permute-start | bytes 1376264 | tf_op jit(solution)/shard_map/ppermute | solution.py:19
  127.6 11.3 %copy-start.1 = (f32[1,4,7,64,64]{3,4,2,1,0:T(8,128)}, f32[1,4,7,64,64]{3,4,2,1,0:T(8,128)S(1)}, u32[]{:S(2)}) copy-start(f32[1,4,7,64,64]{3,4,2,1,0:T(8,128)S(1)} %collective-permute-done.8) | copy-start | bytes 1376260
  131.6 7.2 %copy-start.2 = (f32[1,4,7,64,64]{3,4,2,1,0:T(8,128)}, f32[1,4,7,64,64]{3,4,2,1,0:T(8,128)S(1)}, u32[]{:S(2)}) copy-start(f32[1,4,7,64,64]{3,4,2,1,0:T(8,128)S(1)} %collective-permute-done.9) | copy-start | bytes 1376260
  133.6 23.2 %collective-permute-start.11 = (f32[6,1,7,64,64]{3,4,2,1,0:T(8,128)}, f32[6,1,7,64,64]{3,4,2,1,0:T(8,128)}, u32[]{:S(2)}, u32[]{:S(2)}) collective-permute-start(f32[6,1,7,64,64]{3,4,2,1,0:T(8,128)} %get-tuple-element.14), channel_id=1, source_target_pairs={{0,1},{1,2},{2,3},{3,4},{4,5},{5,6},{6,7},{7,8},{8,9},{9,10},{10,1... | collective-permute-start | bytes 2064392 | tf_op jit(solution)/shard_map/ppermute | solution.py:19
  136.7 21.2 %collective-permute-start.10 = (f32[6,1,7,64,64]{3,4,2,1,0:T(8,128)}, f32[6,1,7,64,64]{3,4,2,1,0:T(8,128)}, u32[]{:S(2)}, u32[]{:S(2)}) collective-permute-start(f32[6,1,7,64,64]{3,4,2,1,0:T(8,128)} %get-tuple-element.13), channel_id=1, source_target_pairs={{1,0},{2,1},{3,2},{4,3},{5,4},{6,5},{7,6},{8,7},{9,8},{10,9},{11,1... | collective-permute-start | bytes 2064392 | tf_op jit(solution)/shard_map/ppermute | solution.py:21
